TPU v7x, 128 devices: a whole 4x4x4 slice. The times are simulated.
128 devices in a mesh: leaf: 16 (over x, y), col: 8 (over z, core).
Axes of the slice: x: 4, y: 4, z: 4, core: 2. Of those that a mesh axis runs over, the one named last changes fastest.
Arguments:
- right_side: float32 [31, 2560, 256], P(None, 'leaf'), may hold values from -6 to 6
- reciprocal_pivot_matrix: bfloat16 [31, 2560, 2560], P(None, 'col', 'leaf'), as said below
- panels: bfloat16 [98, 2560, 2560], P(None, 'leaf', 'col'), may hold values from -0.03125 to 0.03125
- parent: int32 [31], replicated, may hold values from 16 to 30, as said below
Outputs:
- solution: float32 [31, 2560, 256], P(None, 'leaf')
Inputs may be any that keep to these rules, and one draw needn't show every extreme that they name: Supernodes 0 to 15 have parents among 16 to 23, 16 to 23 among 24 to 27, 24 to 27 among 28 and 29, 28 and 29 have parent 30, and entry 30 is 30 itself; each supernode of levels 1 to 4 is the parent of exactly two supernodes of the level below. `reciprocal_pivot_matrix`: each block is lower triangular with a positive diagonal.
All inputs are finite; a program needn't handle non-finite values.
Results may differ from a plain program's by a relative error of at most 0.03.
Values may be sent and summed in bfloat16 or wider, within the bound.
No kernel may reach another device: no remote copies, remote signals or barrier semaphores. Data moves between devices by JAX's collectives and lax.ppermute only.
A program may use at most 192 MiB of HBM per device.

v0:
```python
import jax
import jax.numpy as jnp
import numpy as np
from jax import lax
from jax.sharding import PartitionSpec as P

level_starts = (0, 16, 24, 28, 30)
level_counts = (16, 8, 4, 2, 1)


def pair_table():
    sources = []
    distances = []
    for tree_level in range(5):
        for tree_vertex in range(
            level_starts[tree_level], level_starts[tree_level] + level_counts[tree_level]
        ):
            for distance in range(1, 5 - tree_level):
                sources.append(tree_vertex)
                distances.append(distance)
    return (sources, distances)


def node_level(tree_vertex):
    deepest = 0
    for tree_level in range(5):
        if level_starts[tree_level] <= tree_vertex:
            deepest = tree_level
    return deepest


def pair_offset(tree_level):
    initial_position = 0
    for lower in range(tree_level):
        initial_position = initial_position + level_counts[lower] * (4 - lower)
    return initial_position


def pair_ancestors(parent):
    sources, distances = pair_table()
    climbed = [jnp.arange(parent.shape[0], dtype=jnp.int32)]
    for distance in range(4):
        climbed.append(parent[climbed[-1]])
    return jnp.stack(
        [climbed[distance][source_node] for source_node, distance in zip(sources, distances)]
    )


def forward_products(panel_local, forward_stack, ancestor, pair_list, start_node, node_count):
    sources, distances = pair_table()
    chosen = np.array(pair_list, dtype=np.int32)
    feeders = np.array([sources[node_pairing] for node_pairing in pair_list], dtype=np.int32)
    products = jnp.einsum(
        "sjv,svk->sjk",
        panel_local[chosen],
        forward_stack[feeders],
        preferred_element_type=jnp.float32,
    )
    slots = jnp.arange(node_count, dtype=jnp.int32) + start_node
    onehot = (slots[:, None] == ancestor[chosen][None, :]).astype(jnp.float32)
    return jnp.einsum("kp,par->kar", onehot, products, precision=lax.Precision.HIGHEST)


def solve(right_side, diag_local, panel_local, ancestor):
    sources, distances = pair_table()
    node_total = right_side.shape[0]
    load_vector_count = right_side.shape[2]
    col_rows = diag_local.shape[1]
    leaf_rows = diag_local.shape[2]
    forward_stack = jnp.zeros((node_total, col_rows, load_vector_count), jnp.bfloat16)
    forward_levels = [None] * 5
    for tree_level in range(5):
        start_node = level_starts[tree_level]
        node_count = level_counts[tree_level]
        reduced = right_side[start_node : start_node + node_count]
        if tree_level > 0:
            arriving = [
                node_pairing
                for node_pairing in range(len(sources))
                if node_level(sources[node_pairing]) + distances[node_pairing] == tree_level
            ]
            partial_value = forward_products(
                panel_local, forward_stack, ancestor, arriving, start_node, node_count
            )
            reduced = reduced - lax.psum(partial_value.astype(jnp.bfloat16), "col").astype(
                jnp.float32
            )
        division_count = jnp.einsum(
            "kcl,klr->kcr",
            diag_local[start_node : start_node + node_count],
            reduced.astype(jnp.bfloat16),
            preferred_element_type=jnp.float32,
        )
        forward_value = lax.psum(division_count.astype(jnp.bfloat16), "leaf").astype(jnp.float32)
        forward_levels[tree_level] = forward_value
        forward_stack = forward_stack.at[start_node : start_node + node_count].set(
            forward_value.astype(jnp.bfloat16)
        )
    solution_stack = jnp.zeros((node_total, leaf_rows, load_vector_count), jnp.bfloat16)
    results = [None] * 5
    for tree_level in (4, 3, 2, 1, 0):
        start_node = level_starts[tree_level]
        node_count = level_counts[tree_level]
        corrected = forward_levels[tree_level]
        if tree_level < 4:
            initial_position = pair_offset(tree_level)
            span_pairs = node_count * (4 - tree_level)
            upper_node = solution_stack[ancestor[initial_position : initial_position + span_pairs]]
            products = jnp.einsum(
                "boj,boh->bjh",
                panel_local[initial_position : initial_position + span_pairs],
                upper_node,
                preferred_element_type=jnp.float32,
            )
            partial_value = jnp.sum(
                products.reshape(node_count, 4 - tree_level, col_rows, load_vector_count), axis=1
            )
            corrected = corrected - lax.psum(partial_value.astype(jnp.bfloat16), "leaf").astype(
                jnp.float32
            )
        division_count = jnp.einsum(
            "kcl,kcr->klr",
            diag_local[start_node : start_node + node_count],
            corrected.astype(jnp.bfloat16),
            preferred_element_type=jnp.float32,
        )
        solution = lax.psum(division_count.astype(jnp.bfloat16), "col").astype(jnp.float32)
        results[tree_level] = solution
        solution_stack = solution_stack.at[start_node : start_node + node_count].set(
            solution.astype(jnp.bfloat16)
        )
    return jnp.concatenate(results, axis=0)


def shards(right_side, reciprocal_pivot_matrix, panels, parent):
    ancestor = pair_ancestors(parent)
    return solve(right_side, reciprocal_pivot_matrix, panels, ancestor)


def solution(mesh):
    return jax.shard_map(
        shards,
        mesh=mesh,
        in_specs=(P(None, "leaf", None), P(None, "col", "leaf"), P(None, "leaf", "col"), P()),
        out_specs=P(None, "leaf", None),
        check_vma=False,
    )
```

profile of v0, /device:TPU:0, one launch (start us, length us, event | category | flops | bytes accessed | tf_op | source)
XLA Modules:
  0.0 1465.1 jit_solution(12247454413178244909)
XLA Ops:
  6.5 4.8 convolution_convert_fusion
  18.7 62.5 %stack.204 = s32[98]{0:T(128)S(1)} concatenate(s32[1]{0:T(128)} %get-tuple-element.201, s32[1]{0:T(128)} %get-tuple-element.184, s32[1]{0:T(128)} %get-tuple-element.198, s32[1]{0:T(128)} %get-tuple-element.175, s32[1]{0:T(128)} %get-tuple-element.202, s32[1]{0:T(128)} %get-tuple-element.183, s32[1]{0:T(128)} %get-tuple-element.197, s32[1]{0:T(128)} %get-tuple-element.174, ...), dimensions={0} | concatenate | bytes 784 | tf_op jit(solution)/shard_map/stack | solution.py:44
  81.9 5.4 gather_fusion.7
  87.3 19.3 %all-reduce.21.cloned.1.call-done = bf16[16,320,256]{2,1,0:T(8,128)(2,1)} async-done(((bf16[16,320,256]{2,1,0:T(8,128)(2,1)}), bf16[16,320,256]{2,1,0:T(8,128)(2,1)}) %all-reduce.21.cloned.1.call-update) | async-done | bytes 2621456 | tf_op jit(solution)/shard_map/psum | solution.py:94
  106.7 4.5 scatter.26
  111.2 4.7 gather_fusion.8
  115.9 2.6 fusion.78
  118.5 2.4 fusion.13
  122.0 61.0 %all-reduce.23.cloned.1.call-done = bf16[8,160,256]{2,1,0:T(8,128)(2,1)} async-done(((bf16[8,160,256]{2,1,0:T(8,128)(2,1)}), bf16[8,160,256]{2,1,0:T(8,128)(2,1)}) %all-reduce.23.cloned.1.call-update) | async-done | bytes 655376 | tf_op jit(solution)/shard_map/psum | solution.py:85
  183.0 3.5 fusion.19
  186.9 7.2 gather_fusion.10
  194.8 78.5 %all-reduce.25.cloned.1.call-done = bf16[8,320,256]{2,1,0:T(8,128)(2,1)} async-done(((bf16[8,320,256]{2,1,0:T(8,128)(2,1)}), bf16[8,320,256]{2,1,0:T(8,128)(2,1)}) %all-reduce.25.cloned.1.call-update) | async-done | bytes 1310736 | tf_op jit(solution)/shard_map/psum | solution.py:94
  273.3 2.5 constant_dynamic-update-slice_fusion.10
  275.8 5.2 gather_fusion.11
  281.0 4.2 fusion.79
  285.2 3.6 fusion.8
  289.7 59.9 %all-reduce.27.cloned.1.call-done = bf16[4,160,256]{2,1,0:T(8,128)(2,1)} async-done(((bf16[4,160,256]{2,1,0:T(8,128)(2,1)}), bf16[4,160,256]{2,1,0:T(8,128)(2,1)}) %all-reduce.27.cloned.1.call-update) | async-done | bytes 327696 | tf_op jit(solution)/shard_map/psum | solution.py:85
  349.6 2.6 fusion.24
  352.8 7.3 gather_fusion.13
  360.8 76.0 %all-reduce.29.cloned.1.call-done = bf16[4,320,256]{2,1,0:T(8,128)(2,1)} async-done(((bf16[4,320,256]{2,1,0:T(8,128)(2,1)}), bf16[4,320,256]{2,1,0:T(8,128)(2,1)}) %all-reduce.29.cloned.1.call-update) | async-done | bytes 655376 | tf_op jit(solution)/shard_map/psum | solution.py:94
  436.8 2.0 constant_dynamic-update-slice_fusion.9
  438.8 5.4 gather_fusion.14
  444.2 4.7 fusion.80
  448.9 4.4 fusion.4
  454.0 57.4 %all-reduce.31.cloned.1.call-done = bf16[2,160,256]{2,1,0:T(8,128)(2,1)} async-done(((bf16[2,160,256]{2,1,0:T(8,128)(2,1)}), bf16[2,160,256]{2,1,0:T(8,128)(2,1)}) %all-reduce.31.cloned.1.call-update) | async-done | bytes 163856 | tf_op jit(solution)/shard_map/psum | solution.py:85
  511.4 2.2 fusion.25
  513.8 7.4 gather_fusion.5
  522.0 76.1 %all-reduce.33.cloned.1.call-done = bf16[2,320,256]{2,1,0:T(8,128)(2,1)} async-done(((bf16[2,320,256]{2,1,0:T(8,128)(2,1)}), bf16[2,320,256]{2,1,0:T(8,128)(2,1)}) %all-reduce.33.cloned.1.call-update) | async-done | bytes 327696 | tf_op jit(solution)/shard_map/psum | solution.py:94
  598.1 1.7 constant_dynamic-update-slice_fusion.8
  599.8 5.5 gather_fusion.15
  605.4 5.0 fusion.81
  610.3 4.6 fusion.2
  615.7 54.3 %all-reduce.35.cloned.1.call-done = bf16[1,160,256]{2,1,0:T(8,128)(2,1)} async-done(((bf16[1,160,256]{2,1,0:T(8,128)(2,1)}), bf16[1,160,256]{2,1,0:T(8,128)(2,1)}) %all-reduce.35.cloned.1.call-update) | async-done | bytes 81936 | tf_op jit(solution)/shard_map/psum | solution.py:85
  669.9 2.0 fusion.28
  672.0 84.8 %all-reduce.37.cloned.1.call-done = bf16[320,256]{0,1:T(8,128)(2,1)} async-done(((bf16[320,256]{0,1:T(8,128)(2,1)}), bf16[320,256]{0,1:T(8,128)(2,1)}) %all-reduce.37.cloned.1.call-update) | async-done | bytes 163856 | tf_op jit(solution)/shard_map/psum | solution.py:94
  756.8 1.9 fusion.30
  758.7 54.4 %all-reduce.39.cloned.1.call-done = bf16[1,160,256]{2,1,0:T(8,128)(2,1)} async-done(((bf16[1,160,256]{2,1,0:T(8,128)(2,1)}), bf16[1,160,256]{2,1,0:T(8,128)(2,1)}) %all-reduce.39.cloned.1.call-update) | async-done | bytes 81936 | tf_op jit(solution)/shard_map/psum | solution.py:127
  813.1 1.2 scatter.34
  814.2 1.2 gather_fusion.16
  815.4 2.1 fusion.26
  817.6 5.2 stack.213
  822.9 78.6 %all-reduce.41.cloned.1.call-done = bf16[2,320,256]{2,1,0:T(8,128)(2,1)} async-done(((bf16[2,320,256]{2,1,0:T(8,128)(2,1)}), bf16[2,320,256]{2,1,0:T(8,128)(2,1)}) %all-reduce.41.cloned.1.call-update) | async-done | bytes 327696 | tf_op jit(solution)/shard_map/psum | solution.py:118
  901.4 2.0 fusion.29
  903.6 57.6 %all-reduce.43.cloned.1.call-done = bf16[2,160,256]{2,1,0:T(8,128)(2,1)} async-done(((bf16[2,160,256]{2,1,0:T(8,128)(2,1)}), bf16[2,160,256]{2,1,0:T(8,128)(2,1)}) %all-reduce.43.cloned.1.call-update) | async-done | bytes 163856 | tf_op jit(solution)/shard_map/psum | solution.py:127
  962.1 1.4 gather_fusion.17
  963.5 3.1 bitcast_reduce_fusion.1
  966.7 15.4 %stack.238 = s32[24,1]{0,1:T(1,128)S(1)} concatenate(s32[1,1]{0,1:T(1,128)} %bitcast.34, s32[1,1]{0,1:T(1,128)} %bitcast.35, s32[1,1]{0,1:T(1,128)} %bitcast.36, s32[1,1]{0,1:T(1,128)} %bitcast.37, s32[1,1]{0,1:T(1,128)} %bitcast.38, s32[1,1]{0,1:T(1,128)} %bitcast.39, s32[1,1]{0,1:T(1,128)} %bitcast.40, s32[1,1]{0,1:T(1,128)} %bitcast.41, s32[1,1]{0,1:T(1,128)} %bitcast.42, ...), dimensions={0} | concatenate | bytes 192 | tf_op jit(solution)/shard_map/stack | solution.py:44
  982.1 69.6 %all-reduce.45.cloned.1.call-done = bf16[4,320,256]{2,1,0:T(8,128)(2,1)} async-done(((bf16[4,320,256]{2,1,0:T(8,128)(2,1)}), bf16[4,320,256]{2,1,0:T(8,128)(2,1)}) %all-reduce.45.cloned.1.call-update) | async-done | bytes 655376 | tf_op jit(solution)/shard_map/psum | solution.py:118
  1051.7 2.3 fusion.27
  1054.3 59.6 %all-reduce.47.cloned.1.call-done = bf16[4,160,256]{2,1,0:T(8,128)(2,1)} async-done(((bf16[4,160,256]{2,1,0:T(8,128)(2,1)}), bf16[4,160,256]{2,1,0:T(8,128)(2,1)}) %all-reduce.47.cloned.1.call-update) | async-done | bytes 327696 | tf_op jit(solution)/shard_map/psum | solution.py:127
  1114.9 2.0 gather_fusion.18
  1116.9 6.9 fusion.10
  1123.8 5.3 reduce_sum.32
  1130.3 85.5 %all-reduce.49.cloned.1.call-done = bf16[8,320,256]{2,1,0:T(8,128)(2,1)} async-done(((bf16[8,320,256]{2,1,0:T(8,128)(2,1)}), bf16[8,320,256]{2,1,0:T(8,128)(2,1)}) %all-reduce.49.cloned.1.call-update) | async-done | bytes 1310736 | tf_op jit(solution)/shard_map/psum | solution.py:118
  1215.8 3.4 fusion.23
  1219.3 61.0 %all-reduce.51.cloned.1.call-done = bf16[8,160,256]{2,1,0:T(8,128)(2,1)} async-done(((bf16[8,160,256]{2,1,0:T(8,128)(2,1)}), bf16[8,160,256]{2,1,0:T(8,128)(2,1)}) %all-reduce.51.cloned.1.call-update) | async-done | bytes 655376 | tf_op jit(solution)/shard_map/psum | solution.py:127
  1280.3 1.1 constant_dynamic-update-slice_fusion.5
  1281.5 3.2 gather_fusion.19
  1284.7 8.7 bitcast_reduce_fusion
  1293.5 91.8 %all-reduce.53.cloned.1.call-done = bf16[16,320,256]{2,1,0:T(8,128)(2,1)} async-done(((bf16[16,320,256]{2,1,0:T(8,128)(2,1)}), bf16[16,320,256]{2,1,0:T(8,128)(2,1)}) %all-reduce.53.cloned.1.call-update) | async-done | bytes 2621456 | tf_op jit(solution)/shard_map/psum | solution.py:118
  1385.3 5.1 fusion.20
  1390.4 63.1 %all-reduce.55.cloned.1.call-done = bf16[16,160,256]{2,1,0:T(8,128)(2,1)} async-done(((bf16[16,160,256]{2,1,0:T(8,128)(2,1)}), bf16[16,160,256]{2,1,0:T(8,128)(2,1)}) %all-reduce.55.cloned.1.call-update) | async-done | bytes 1310736 | tf_op jit(solution)/shard_map/psum | solution.py:127
  1453.5 1.4 constant_dynamic-update-slice_fusion.4
  1455.1 2.9 concatenate.84
  (114 shorter events, 18.5 us)
Async XLA Ops:
  6.5 4.9 copy-start
  6.5 100.1 %all-reduce.21.cloned.1.call-start = ((), (), s32[]{:S(2)}) async-start(), calls=%async_computation | async-start | bytes 5242880 | tf_op jit(solution)/shard_map/psum | solution.py:94
  11.4 171.6 %all-reduce.23.cloned.1.call-start = ((), (), s32[]{:S(2)}) async-start(), calls=%async_computation.1 | async-start | bytes 1310720 | tf_op jit(solution)/shard_map/psum | solution.py:85
  120.9 66.0 %copy-start.10 = (s32[24]{0:T(128)S(1)}, s32[24]{0:T(128)}, u32[]{:S(2)}) copy-start(s32[24]{0:T(128)} %constant.265) | copy-start | bytes 292
  122.0 151.3 %all-reduce.25.cloned.1.call-start = ((), (), s32[]{:S(2)}) async-start(), calls=%async_computation.2 | async-start | bytes 2621440 | tf_op jit(solution)/shard_map/psum | solution.py:94
  186.6 163.1 %all-reduce.27.cloned.1.call-start = ((), (), s32[]{:S(2)}) async-start(), calls=%async_computation.3 | async-start | bytes 655360 | tf_op jit(solution)/shard_map/psum | solution.py:85
  285.2 67.6 %copy-start.9 = (s32[28]{0:T(128)S(1)}, s32[28]{0:T(128)}, u32[]{:S(2)}) copy-start(s32[28]{0:T(128)} %constant.267) | copy-start | bytes 340
  289.6 147.2 %all-reduce.29.cloned.1.call-start = ((), (), s32[]{:S(2)}) async-start(), calls=%async_computation.4 | async-start | bytes 1310720 | tf_op jit(solution)/shard_map/psum | solution.py:94
  352.2 159.2 %all-reduce.31.cloned.1.call-start = ((), (), s32[]{:S(2)}) async-start(), calls=%async_computation.5 | async-start | bytes 327680 | tf_op jit(solution)/shard_map/psum | solution.py:85
  448.9 64.9 %copy-start.8 = (s32[30]{0:T(128)S(1)}, s32[30]{0:T(128)}, u32[]{:S(2)}) copy-start(s32[30]{0:T(128)} %constant.263) | copy-start | bytes 364
  454.0 144.1 %all-reduce.33.cloned.1.call-start = ((), (), s32[]{:S(2)}) async-start(), calls=%async_computation.6 | async-start | bytes 655360 | tf_op jit(solution)/shard_map/psum | solution.py:94
  513.6 156.4 %all-reduce.35.cloned.1.call-start = ((), (), s32[]{:S(2)}) async-start(), calls=%async_computation.7 | async-start | bytes 163840 | tf_op jit(solution)/shard_map/psum | solution.py:85
  614.9 286.5 %copy-start.5 = (bf16[2,320,256]{2,1,0:T(8,128)(2,1)S(1)}, bf16[2,320,256]{2,1,0:T(8,128)(2,1)}, u32[]{:S(2)}) copy-start(bf16[2,320,256]{2,1,0:T(8,128)(2,1)} %all-reduce.33.cloned.1.call-done) | copy-start | bytes 983044
  615.6 141.1 %all-reduce.37.cloned.1.call-start = ((), (), s32[]{:S(2)}) async-start(), calls=%async_computation.8 | async-start | bytes 393216 | tf_op jit(solution)/shard_map/psum | solution.py:94
  671.9 141.1 %all-reduce.39.cloned.1.call-start = ((), (), s32[]{:S(2)}) async-start(), calls=%async_computation.9 | async-start | bytes 163840 | tf_op jit(solution)/shard_map/psum | solution.py:127
  758.6 142.8 %all-reduce.41.cloned.1.call-start = ((), (), s32[]{:S(2)}) async-start(), calls=%async_computation.10 | async-start | bytes 655360 | tf_op jit(solution)/shard_map/psum | solution.py:118
  815.4 236.2 %copy-start.2 = (bf16[4,320,256]{2,1,0:T(8,128)(2,1)S(1)}, bf16[4,320,256]{2,1,0:T(8,128)(2,1)}, u32[]{:S(2)}) copy-start(bf16[4,320,256]{2,1,0:T(8,128)(2,1)} %all-reduce.29.cloned.1.call-done) | copy-start | bytes 1966084
  817.6 143.6 %all-reduce.43.cloned.1.call-start = ((), (), s32[]{:S(2)}) async-start(), calls=%async_computation.11 | async-start | bytes 327680 | tf_op jit(solution)/shard_map/psum | solution.py:127
  903.5 148.2 %all-reduce.45.cloned.1.call-start = ((), (), s32[]{:S(2)}) async-start(), calls=%async_computation.12 | async-start | bytes 1310720 | tf_op jit(solution)/shard_map/psum | solution.py:118
  966.6 147.3 %all-reduce.47.cloned.1.call-start = ((), (), s32[]{:S(2)}) async-start(), calls=%async_computation.13 | async-start | bytes 655360 | tf_op jit(solution)/shard_map/psum | solution.py:127
  1054.1 161.8 %all-reduce.49.cloned.1.call-start = ((), (), s32[]{:S(2)}) async-start(), calls=%async_computation.14 | async-start | bytes 2621440 | tf_op jit(solution)/shard_map/psum | solution.py:118
  1129.2 151.2 %all-reduce.51.cloned.1.call-start = ((), (), s32[]{:S(2)}) async-start(), calls=%async_computation.15 | async-start | bytes 1310720 | tf_op jit(solution)/shard_map/psum | solution.py:127
  1219.2 166.1 %all-reduce.53.cloned.1.call-start = ((), (), s32[]{:S(2)}) async-start(), calls=%async_computation.16 | async-start | bytes 5242880 | tf_op jit(solution)/shard_map/psum | solution.py:118
  1293.4 160.1 %all-reduce.55.cloned.1.call-start = ((), (), s32[]{:S(2)}) async-start(), calls=%async_computation.17 | async-start | bytes 2621440 | tf_op jit(solution)/shard_map/psum | solution.py:127
  1390.4 64.5 %copy-start.3 = (bf16[8,160,256]{2,1,0:T(8,128)(2,1)S(1)}, bf16[8,160,256]{2,1,0:T(8,128)(2,1)}, u32[]{:S(2)}) copy-start(bf16[8,160,256]{2,1,0:T(8,128)(2,1)} %all-reduce.51.cloned.1.call-done) | copy-start | bytes 1966084
  1390.4 64.6 %copy-start.4 = (bf16[4,160,256]{2,1,0:T(8,128)(2,1)S(1)}, bf16[4,160,256]{2,1,0:T(8,128)(2,1)}, u32[]{:S(2)}) copy-start(bf16[4,160,256]{2,1,0:T(8,128)(2,1)} %all-reduce.47.cloned.1.call-done) | copy-start | bytes 983044
  1390.4 64.6 %copy-start.6 = (bf16[2,160,256]{2,1,0:T(8,128)(2,1)S(1)}, bf16[2,160,256]{2,1,0:T(8,128)(2,1)}, u32[]{:S(2)}) copy-start(bf16[2,160,256]{2,1,0:T(8,128)(2,1)} %all-reduce.43.cloned.1.call-done) | copy-start | bytes 491524
  1390.4 64.6 %copy-start.7 = (bf16[1,160,256]{2,1,0:T(8,128)(2,1)S(1)}, bf16[1,160,256]{2,1,0:T(8,128)(2,1)}, u32[]{:S(2)}) copy-start(bf16[1,160,256]{2,1,0:T(8,128)(2,1)} %all-reduce.39.cloned.1.call-done) | copy-start | bytes 245764
  1455.0 3.0 copy-start.1
Sparse Core Ops, SparseCore 0:
  11.5 95.1 all-reduce.20
  122.1 60.9 all-reduce.22
  186.7 86.5 all-reduce.24
  289.7 59.8 all-reduce.26
  352.7 84.0 all-reduce.28
  454.1 57.2 all-reduce.30
  514.9 83.1 all-reduce.32
  615.7 54.1 all-reduce.34
  673.1 83.5 all-reduce.36
  758.9 54.0 all-reduce.38
  817.7 83.6 all-reduce.40
  903.7 57.3 all-reduce.42
  966.7 84.9 all-reduce.44
  1054.2 59.7 all-reduce.46
  1129.3 86.4 all-reduce.48
  1219.4 60.9 all-reduce.50
  1293.5 91.7 all-reduce.52
  1390.5 62.9 all-reduce.54
where the time goes:
time: 1470 us
  waiting for transfers between devices  1190 us (81%)
  local copies, waits for them, and re-layouts  170 us (12%)
  matrix products  82 us (6%)
    psum x5, waiting for transfers between devices, solve(): lax.psum(division_count.astype(jnp.bfloat16), 'leaf').astype(jnp.float32)  335 us
    psum x4, waiting for transfers between devices, solve(): lax.psum(partial_value.astype(jnp.bfloat16), 'leaf').astype(jnp.float32)  326 us
    psum x5, waiting for transfers between devices, solve(): lax.psum(division_count.astype(jnp.bfloat16), 'col').astype(jnp.float32)  296 us
    psum x4, waiting for transfers between devices, solve(): lax.psum(partial_value.astype(jnp.bfloat16), 'col').astype(jnp.float32)  233 us
    another operation x4, local copies, waits for them, and re-layouts, pair_ancestors(): jnp.stack([climbed[distance][source_node] for source_node, distance in zi...  84.2 us
  transfers between devices with their start and end apart: 18, of which 18 were waited for; matrix products, arithmetic and copies ran while one was open for 8% of the time, Pallas kernels for 0%

commit v1 on v0

--- a/solution.py
+++ b/solution.py
@@ -91,7 +91,9 @@
             reduced.astype(jnp.bfloat16),
             preferred_element_type=jnp.float32,
         )
-        forward_value = lax.psum(division_count.astype(jnp.bfloat16), "leaf").astype(jnp.float32)
+        forward_value = jnp.sum(
+            lax.all_gather(division_count.astype(jnp.bfloat16), "leaf"), axis=0
+        ).astype(jnp.float32)
         forward_levels[tree_level] = forward_value
         forward_stack = forward_stack.at[start_node : start_node + node_count].set(
             forward_value.astype(jnp.bfloat16)

time: 1470 us -> 1630 us (1.11)
  waiting for transfers between devices: 1190 us -> 1310 us
  other arithmetic: 8.48 us -> 50.6 us
    all_gather x0 -> x5, waiting for transfers between devices: none -> 453 us  [solve(): lax.all_gather(division_count.astype(jnp.bfloat16), 'leaf')]
    psum x5 -> x0, waiting for transfers between devices: 335 us -> none  [solve(): lax.psum(division_count.astype(jnp.bfloat16), 'leaf').astype(jnp.float32)]
    reduce_sum x0 -> x5, other arithmetic: none -> 38.9 us  [solve(): jnp.sum(lax.all_gather(division_count.astype(jnp.bfloat16), 'leaf'), axis=0)]
where the time goes in v1:
time: 1630 us; the launch traced here: 1620 us
  waiting for transfers between devices  1310 us (80%)
  local copies, waits for them, and re-layouts  167 us (10%)
  matrix products  82.6 us (5%)
  other arithmetic  50.6 us (3%)
    all_gather x5, waiting for transfers between devices, solve(): lax.all_gather(division_count.astype(jnp.bfloat16), 'leaf')  453 us
    psum x4, waiting for transfers between devices, solve(): lax.psum(partial_value.astype(jnp.bfloat16), 'leaf').astype(jnp.float32)  326 us
    psum x5, waiting for transfers between devices, solve(): lax.psum(division_count.astype(jnp.bfloat16), 'col').astype(jnp.float32)  295 us
    psum x4, waiting for transfers between devices, solve(): lax.psum(partial_value.astype(jnp.bfloat16), 'col').astype(jnp.float32)  234 us
    another operation x4, local copies, waits for them, and re-layouts, pair_ancestors(): jnp.stack([climbed[distance][source_node] for source_node, distance in zi...  82.7 us
    reduce_sum x5, other arithmetic, solve(): jnp.sum(lax.all_gather(division_count.astype(jnp.bfloat16), 'leaf'), axis=0)  38.9 us
  transfers between devices with their start and end apart: 18, of which 18 were waited for; matrix products, arithmetic and copies ran while one was open for 8% of the time, Pallas kernels for 0%

profile of v1, /device:TPU:0, one launch (start us, length us, event | category | flops | bytes accessed | tf_op | source)
XLA Modules:
  0.0 1624.9 jit_solution(7201858033078469960)
XLA Ops:
  6.5 4.8 convolution_convert_fusion
  18.7 61.5 %stack.204 = s32[98]{0:T(128)S(1)} concatenate(s32[1]{0:T(128)} %get-tuple-element.207, s32[1]{0:T(128)} %get-tuple-element.184, s32[1]{0:T(128)} %get-tuple-element.198, s32[1]{0:T(128)} %get-tuple-element.175, s32[1]{0:T(128)} %get-tuple-element.208, s32[1]{0:T(128)} %get-tuple-element.183, s32[1]{0:T(128)} %get-tuple-element.197, s32[1]{0:T(128)} %get-tuple-element.174, ...), dimensions={0} | concatenate | bytes 784 | tf_op jit(solution)/shard_map/stack | solution.py:44
  80.9 8.7 gather_fusion.7
  89.6 164.2 %all-gather.11.cloned.1.call-done = bf16[256,320,256]{2,1,0:T(8,128)(2,1)} async-done(((bf16[16,320,256]{2,1,0:T(8,128)(2,1)}), bf16[256,320,256]{2,1,0:T(8,128)(2,1)}) %all-gather.11.cloned.1.call-update) | async-done | bytes 41943056 | tf_op jit(solution)/shard_map/all_gather | solution.py:95
  253.8 15.8 reduce_sum.91
  269.7 4.5 scatter.26
  274.2 4.6 gather_fusion.8
  278.9 2.6 fusion.88
  281.5 3.4 fusion.23
  285.0 61.4 %all-reduce.16.cloned.1.call-done = bf16[8,160,256]{2,0,1:T(8,128)(2,1)} async-done(((bf16[8,160,256]{2,0,1:T(8,128)(2,1)}), bf16[8,160,256]{2,0,1:T(8,128)(2,1)}) %all-reduce.16.cloned.1.call-update) | async-done | bytes 655376 | tf_op jit(solution)/shard_map/psum | solution.py:85
  346.4 1.8 fusion.26
  348.2 3.0 fusion.19
  351.4 7.2 gather_fusion.10
  359.3 123.7 %all-gather.13.cloned.1.call-done = bf16[128,320,256]{2,1,0:T(8,128)(2,1)} async-done(((bf16[8,320,256]{2,1,0:T(8,128)(2,1)}), bf16[128,320,256]{2,1,0:T(8,128)(2,1)}) %all-gather.13.cloned.1.call-update) | async-done | bytes 20971536 | tf_op jit(solution)/shard_map/all_gather | solution.py:95
  483.0 11.6 reduce_sum.92
  495.8 5.2 gather_fusion.11
  501.1 4.2 fusion.89
  505.3 4.3 fusion.29
  509.6 60.3 %all-reduce.18.cloned.1.call-done = bf16[4,160,256]{2,0,1:T(4,128)(2,1)} async-done(((bf16[4,160,256]{2,0,1:T(4,128)(2,1)}), bf16[4,160,256]{2,0,1:T(4,128)(2,1)}) %all-reduce.18.cloned.1.call-update) | async-done | bytes 327696 | tf_op jit(solution)/shard_map/psum | solution.py:85
  570.0 1.5 fusion.44
  571.5 2.3 fusion.28
  574.1 7.4 gather_fusion.13
  582.2 71.0 %all-gather.15.cloned.1.call-done = bf16[64,320,256]{2,1,0:T(8,128)(2,1)} async-done(((bf16[4,320,256]{2,1,0:T(8,128)(2,1)}), bf16[64,320,256]{2,1,0:T(8,128)(2,1)}) %all-gather.15.cloned.1.call-update) | async-done | bytes 10485776 | tf_op jit(solution)/shard_map/all_gather | solution.py:95
  653.2 6.0 reduce_sum.93
  660.1 5.4 gather_fusion.14
  665.5 4.7 fusion.90
  670.2 4.4 fusion.4
  675.4 57.8 %all-reduce.20.cloned.1.call-done = bf16[2,160,256]{2,1,0:T(8,128)(2,1)} async-done(((bf16[2,160,256]{2,1,0:T(8,128)(2,1)}), bf16[2,160,256]{2,1,0:T(8,128)(2,1)}) %all-reduce.20.cloned.1.call-update) | async-done | bytes 163856 | tf_op jit(solution)/shard_map/psum | solution.py:85
  733.2 2.2 fusion.32
  735.8 7.5 gather_fusion.5
  744.0 47.6 %all-gather.17.cloned.1.call-done = bf16[32,320,256]{2,1,0:T(8,128)(2,1)} async-done(((bf16[2,320,256]{2,1,0:T(8,128)(2,1)}), bf16[32,320,256]{2,1,0:T(8,128)(2,1)}) %all-gather.17.cloned.1.call-update) | async-done | bytes 5242896 | tf_op jit(solution)/shard_map/all_gather | solution.py:95
  791.6 3.3 reduce_sum.94
  795.7 5.5 gather_fusion.15
  801.3 5.0 fusion.91
  806.2 4.6 fusion.2
  811.5 54.6 %all-reduce.22.cloned.1.call-done = bf16[1,160,256]{2,1,0:T(8,128)(2,1)} async-done(((bf16[1,160,256]{2,1,0:T(8,128)(2,1)}), bf16[1,160,256]{2,1,0:T(8,128)(2,1)}) %all-reduce.22.cloned.1.call-update) | async-done | bytes 81936 | tf_op jit(solution)/shard_map/psum | solution.py:85
  866.1 1.9 fusion.36
  868.1 47.0 %all-gather.19.cloned.1.call-done = bf16[5120,256]{1,0:T(8,128)(2,1)} async-done(((bf16[320,256]{1,0:T(8,128)(2,1)}), bf16[5120,256]{1,0:T(8,128)(2,1)}) %all-gather.19.cloned.1.call-update) | async-done | bytes 2621456 | tf_op jit(solution)/shard_map/all_gather | solution.py:95
  915.1 2.1 reduce.22
  917.2 1.7 fusion.37
  919.0 54.1 %all-reduce.24.cloned.1.call-done = bf16[1,160,256]{2,1,0:T(8,128)(2,1)} async-done(((bf16[1,160,256]{2,1,0:T(8,128)(2,1)}), bf16[1,160,256]{2,1,0:T(8,128)(2,1)}) %all-reduce.24.cloned.1.call-update) | async-done | bytes 81936 | tf_op jit(solution)/shard_map/psum | solution.py:129
  975.5 2.1 fusion.33
  977.6 5.2 stack.213
  982.8 78.6 %all-reduce.26.cloned.1.call-done = bf16[2,320,256]{2,1,0:T(8,128)(2,1)} async-done(((bf16[2,320,256]{2,1,0:T(8,128)(2,1)}), bf16[2,320,256]{2,1,0:T(8,128)(2,1)}) %all-reduce.26.cloned.1.call-update) | async-done | bytes 327696 | tf_op jit(solution)/shard_map/psum | solution.py:120
  1061.4 2.0 fusion.35
  1063.6 57.5 %all-reduce.28.cloned.1.call-done = bf16[2,160,256]{2,1,0:T(8,128)(2,1)} async-done(((bf16[2,160,256]{2,1,0:T(8,128)(2,1)}), bf16[2,160,256]{2,1,0:T(8,128)(2,1)}) %all-reduce.28.cloned.1.call-update) | async-done | bytes 163856 | tf_op jit(solution)/shard_map/psum | solution.py:129
  1122.0 1.4 gather_fusion.17
  1123.4 3.1 bitcast_reduce_fusion.1
  1126.5 15.0 stack.238
  1141.5 70.1 %all-reduce.30.cloned.1.call-done = bf16[4,320,256]{2,1,0:T(8,128)(2,1)} async-done(((bf16[4,320,256]{2,1,0:T(8,128)(2,1)}), bf16[4,320,256]{2,1,0:T(8,128)(2,1)}) %all-reduce.30.cloned.1.call-update) | async-done | bytes 655376 | tf_op jit(solution)/shard_map/psum | solution.py:120
  1211.6 2.3 fusion.34
  1214.2 59.6 %all-reduce.32.cloned.1.call-done = bf16[4,160,256]{2,1,0:T(8,128)(2,1)} async-done(((bf16[4,160,256]{2,1,0:T(8,128)(2,1)}), bf16[4,160,256]{2,1,0:T(8,128)(2,1)}) %all-reduce.32.cloned.1.call-update) | async-done | bytes 327696 | tf_op jit(solution)/shard_map/psum | solution.py:129
  1274.8 2.0 gather_fusion.18
  1276.8 6.9 fusion.10
  1283.7 5.3 reduce_sum.97
  1290.2 85.5 %all-reduce.34.cloned.1.call-done = bf16[8,320,256]{2,1,0:T(8,128)(2,1)} async-done(((bf16[8,320,256]{2,1,0:T(8,128)(2,1)}), bf16[8,320,256]{2,1,0:T(8,128)(2,1)}) %all-reduce.34.cloned.1.call-update) | async-done | bytes 1310736 | tf_op jit(solution)/shard_map/psum | solution.py:120
  1375.7 3.4 fusion.27
  1379.2 61.0 %all-reduce.36.cloned.1.call-done = bf16[8,160,256]{2,1,0:T(8,128)(2,1)} async-done(((bf16[8,160,256]{2,1,0:T(8,128)(2,1)}), bf16[8,160,256]{2,1,0:T(8,128)(2,1)}) %all-reduce.36.cloned.1.call-update) | async-done | bytes 655376 | tf_op jit(solution)/shard_map/psum | solution.py:129
  1441.3 3.2 gather_fusion.19
  1444.5 8.7 bitcast_reduce_fusion
  1453.3 91.9 %all-reduce.38.cloned.1.call-done = bf16[16,320,256]{2,1,0:T(8,128)(2,1)} async-done(((bf16[16,320,256]{2,1,0:T(8,128)(2,1)}), bf16[16,320,256]{2,1,0:T(8,128)(2,1)}) %all-reduce.38.cloned.1.call-update) | async-done | bytes 2621456 | tf_op jit(solution)/shard_map/psum | solution.py:120
  1545.2 5.1 fusion.20
  1550.3 63.1 %all-reduce.40.cloned.1.call-done = bf16[16,160,256]{2,1,0:T(8,128)(2,1)} async-done(((bf16[16,160,256]{2,1,0:T(8,128)(2,1)}), bf16[16,160,256]{2,1,0:T(8,128)(2,1)}) %all-reduce.40.cloned.1.call-update) | async-done | bytes 1310736 | tf_op jit(solution)/shard_map/psum | solution.py:129
  1615.0 2.9 concatenate.84
  (118 shorter events, 24.3 us)
Async XLA Ops:
  6.5 5.0 copy-start
  6.5 247.3 %all-gather.11.cloned.1.call-start = ((), (), s32[]{:S(2)}) async-start(), calls=%async_computation.13 | async-start | bytes 44564480 | tf_op jit(solution)/shard_map/all_gather | solution.py:95
  11.4 68.8 %copy-start.9 = (s32[30]{0:T(128)S(1)}, s32[30]{0:T(128)}, u32[]{:S(2)}) copy-start(s32[30]{0:T(128)} %constant.268) | copy-start | bytes 364
  11.4 78.2 %copy-start.8 = (s32[24]{0:T(128)S(1)}, s32[24]{0:T(128)}, u32[]{:S(2)}) copy-start(s32[24]{0:T(128)} %constant.270) | copy-start | bytes 292
  11.4 335.0 %all-reduce.16.cloned.1.call-start = ((), (), s32[]{:S(2)}) async-start(), calls=%async_computation | async-start | bytes 1310720 | tf_op jit(solution)/shard_map/psum | solution.py:85
  281.5 64.9 %slice-start = ((f32[31,160,256]{2,1,0:T(8,128)}), f32[8,160,256]{2,1,0:T(8,128)S(1)}, s32[]{:S(2)}) async-start(f32[31,160,256]{2,1,0:T(8,128)} %param.40), calls=%async_computation.18 | async-start | bytes 2621440 | tf_op jit(solution)/shard_map/slice | solution.py:75
  284.9 198.1 %all-gather.13.cloned.1.call-start = ((), (), s32[]{:S(2)}) async-start(), calls=%async_computation.14 | async-start | bytes 22282240 | tf_op jit(solution)/shard_map/all_gather | solution.py:95
  351.2 8.1 copy-start.7
  351.2 218.8 %all-reduce.18.cloned.1.call-start = ((), (), s32[]{:S(2)}) async-start(), calls=%async_computation.1 | async-start | bytes 655360 | tf_op jit(solution)/shard_map/psum | solution.py:85
  494.6 6.5 copy-start.2
  505.3 64.7 %slice-start.1 = ((f32[31,160,256]{2,1,0:T(8,128)}), f32[4,160,256]{2,1,0:T(8,128)S(1)}, s32[]{:S(2)}) async-start(f32[31,160,256]{2,1,0:T(8,128)} %param.40), calls=%async_computation.19 | async-start | bytes 1310720 | tf_op jit(solution)/shard_map/slice | solution.py:75
  509.6 143.6 %all-gather.15.cloned.1.call-start = ((), (), s32[]{:S(2)}) async-start(), calls=%async_computation.15 | async-start | bytes 11141120 | tf_op jit(solution)/shard_map/all_gather | solution.py:95
  573.8 159.4 %all-reduce.20.cloned.1.call-start = ((), (), s32[]{:S(2)}) async-start(), calls=%async_computation.2 | async-start | bytes 327680 | tf_op jit(solution)/shard_map/psum | solution.py:85
  675.3 116.3 %all-gather.17.cloned.1.call-start = ((), (), s32[]{:S(2)}) async-start(), calls=%async_computation.16 | async-start | bytes 5570560 | tf_op jit(solution)/shard_map/all_gather | solution.py:95
  735.4 130.7 %all-reduce.22.cloned.1.call-start = ((), (), s32[]{:S(2)}) async-start(), calls=%async_computation.3 | async-start | bytes 163840 | tf_op jit(solution)/shard_map/psum | solution.py:85
  811.5 103.6 %all-gather.19.cloned.1.call-start = ((), (), s32[]{:S(2)}) async-start(), calls=%async_computation.17 | async-start | bytes 2785280 | tf_op jit(solution)/shard_map/all_gather | solution.py:95
  868.1 105.0 %all-reduce.24.cloned.1.call-start = ((), (), s32[]{:S(2)}) async-start(), calls=%async_computation.4 | async-start | bytes 163840 | tf_op jit(solution)/shard_map/psum | solution.py:129
  919.0 142.5 %all-reduce.26.cloned.1.call-start = ((), (), s32[]{:S(2)}) async-start(), calls=%async_computation.5 | async-start | bytes 655360 | tf_op jit(solution)/shard_map/psum | solution.py:120
  977.6 143.5 %all-reduce.28.cloned.1.call-start = ((), (), s32[]{:S(2)}) async-start(), calls=%async_computation.6 | async-start | bytes 327680 | tf_op jit(solution)/shard_map/psum | solution.py:129
  1063.5 148.1 %all-reduce.30.cloned.1.call-start = ((), (), s32[]{:S(2)}) async-start(), calls=%async_computation.7 | async-start | bytes 1310720 | tf_op jit(solution)/shard_map/psum | solution.py:120
  1126.5 147.3 %all-reduce.32.cloned.1.call-start = ((), (), s32[]{:S(2)}) async-start(), calls=%async_computation.8 | async-start | bytes 655360 | tf_op jit(solution)/shard_map/psum | solution.py:129
  1213.9 161.8 %all-reduce.34.cloned.1.call-start = ((), (), s32[]{:S(2)}) async-start(), calls=%async_computation.9 | async-start | bytes 2621440 | tf_op jit(solution)/shard_map/psum | solution.py:120
  1289.0 151.2 %all-reduce.36.cloned.1.call-start = ((), (), s32[]{:S(2)}) async-start(), calls=%async_computation.10 | async-start | bytes 1310720 | tf_op jit(solution)/shard_map/psum | solution.py:129
  1379.1 166.1 %all-reduce.38.cloned.1.call-start = ((), (), s32[]{:S(2)}) async-start(), calls=%async_computation.11 | async-start | bytes 5242880 | tf_op jit(solution)/shard_map/psum | solution.py:120
  1453.3 160.1 %all-reduce.40.cloned.1.call-start = ((), (), s32[]{:S(2)}) async-start(), calls=%async_computation.12 | async-start | bytes 2621440 | tf_op jit(solution)/shard_map/psum | solution.py:129
  1550.3 64.5 %copy-start.3 = (bf16[8,160,256]{2,1,0:T(8,128)(2,1)S(1)}, bf16[8,160,256]{2,1,0:T(8,128)(2,1)}, u32[]{:S(2)}) copy-start(bf16[8,160,256]{2,1,0:T(8,128)(2,1)} %all-reduce.36.cloned.1.call-done) | copy-start | bytes 1966084
  1550.3 64.6 %copy-start.4 = (bf16[4,160,256]{2,1,0:T(8,128)(2,1)S(1)}, bf16[4,160,256]{2,1,0:T(8,128)(2,1)}, u32[]{:S(2)}) copy-start(bf16[4,160,256]{2,1,0:T(8,128)(2,1)} %all-reduce.32.cloned.1.call-done) | copy-start | bytes 983044
  1550.3 64.6 %copy-start.5 = (bf16[2,160,256]{2,1,0:T(8,128)(2,1)S(1)}, bf16[2,160,256]{2,1,0:T(8,128)(2,1)}, u32[]{:S(2)}) copy-start(bf16[2,160,256]{2,1,0:T(8,128)(2,1)} %all-reduce.28.cloned.1.call-done) | copy-start | bytes 491524
  1550.3 64.6 %copy-start.6 = (bf16[1,160,256]{2,1,0:T(8,128)(2,1)S(1)}, bf16[1,160,256]{2,1,0:T(8,128)(2,1)}, u32[]{:S(2)}) copy-start(bf16[1,160,256]{2,1,0:T(8,128)(2,1)} %all-reduce.24.cloned.1.call-done) | copy-start | bytes 245764
  1614.9 3.0 copy-start.1
Sparse Core Ops, SparseCore 0:
  11.5 242.2 all-gather.10
  285.0 61.2 all-reduce.15
  351.3 131.6 all-gather.12
  509.7 60.2 all-reduce.17
  573.9 79.2 all-gather.14
  675.4 57.6 all-reduce.19
  735.5 56.0 all-gather.16
  811.6 54.4 all-reduce.21
  868.5 46.5 all-gather.18
  919.1 53.9 all-reduce.23
  977.7 83.6 all-reduce.25
  1063.6 57.3 all-reduce.27
  1126.6 84.8 all-reduce.29
  1214.0 59.7 all-reduce.31
  1289.1 86.5 all-reduce.33
  1379.2 60.9 all-reduce.35
  1453.4 91.7 all-reduce.37
  1550.5 62.8 all-reduce.39
